TPU v7x, 32 devices: a whole 2x2x4 slice. The times are simulated.
32 devices in a mesh: group: 2 (over x), strip: 16 (over z, y, core).
Axes of the slice: x: 2, y: 2, z: 4, core: 2. Of those that a mesh axis runs over, the one named last changes fastest.
Arguments:
- strip_fields: float32 [3, 64, 128, 128], P(None, ('group', 'strip')), may hold values from -18 to 18
- strip_riser: int32 [64, 1], P('group'), may hold values from 0 to 3; in each aligned block of 2 rows (0 to 1, 2 to 3, ...) at most 2 rows name the same one
- strip_node: int32 [64], P('group'), may hold values from 0 to 1023
- riser_owner: int32 [2, 4], P('group'), may hold values from 0 to 15, as said below
- pivot_inv: float32 [32, 8, 128, 128], P(('group', 'strip')), may hold values from -0.2 to 1
- lower_block: float32 [32, 7, 128, 128], P(('group', 'strip')), may hold values from -0.109375 to 0.109375
- upper_block: float32 [32, 7, 128, 128], P(('group', 'strip')), may hold values from -0.109375 to 0.109375
Outputs:
- vorticity: float32 [64, 128, 128], P(('group', 'strip'))
- displacement: float32 [32, 16, 1024], P(('group', 'strip'))
Inputs may be any that keep to these rules, and one draw needn't show every extreme that they name: `strip_riser`: in each aligned block of 2 strips (the strips of one device) no riser is named more than 2 times, and some block names one riser exactly 2 times. `riser_owner`: the 4 owners in a row are distinct devices.
All inputs are finite; a program needn't handle non-finite values.
Results may differ from a plain program's by a relative error of at most 0.0003.
Values sent between devices are 32-bit elements; how exact they have to be, the bound alone decides.
No kernel may reach another device: no remote copies, remote signals or barrier semaphores. Data moves between devices by JAX's collectives and lax.ppermute only.
A program may use at most 64 MiB of HBM per device.

v0:
```python
import jax
import jax.numpy as jnp
from jax import lax
from jax.sharding import PartitionSpec as P

NSUB = 8
COUPLED = 2
TIME_STEP = 0.25
VISCOSITY = 0.05
COUPLING = 0.5
EXACT_DOT = lax.Precision.HIGHEST


def make_kernels(grid_cells):
    centre = jnp.arange(grid_cells, dtype=jnp.float32) - grid_cells / 2.0 + 0.5
    near_x = (centre / (grid_cells / 16.0))[None, :]
    near_y = (centre / (grid_cells / 16.0))[:, None]
    bell_near = jnp.exp(-(near_x * near_x + near_y * near_y) / 2.0)
    source_x = -near_x * bell_near
    source_y = -near_y * bell_near
    wide_x = (centre / (grid_cells / 8.0))[None, :]
    wide_y = (centre / (grid_cells / 8.0))[:, None]
    bell_wide = jnp.exp(-(wide_x * wide_x + wide_y * wide_y) / 2.0)
    lift_kernel = -wide_x * bell_wide
    drag_kernel = wide_y * bell_wide
    lift_kernel = lift_kernel / jnp.sqrt(jnp.sum(lift_kernel * lift_kernel))
    drag_kernel = drag_kernel / jnp.sqrt(jnp.sum(drag_kernel * drag_kernel))
    return (source_x, source_y, lift_kernel, drag_kernel)


def strip_step(vorticity, flow_x, flow_y, motion, kernels, substeps):
    source_x, source_y, lift_kernel, drag_kernel = kernels
    halves = motion.reshape(motion.shape[0], 2, substeps)
    earlier = jnp.concatenate([jnp.zeros_like(halves[:, :, :1]), halves[:, :, :-1]], axis=2)
    velocity = halves - earlier
    lift_rows = []
    drag_rows = []
    for substep in range(substeps):
        right_cell = jnp.roll(vorticity, -1, axis=2)
        left_cell = jnp.roll(vorticity, 1, axis=2)
        upper_cell = jnp.roll(vorticity, -1, axis=1)
        lower_cell = jnp.roll(vorticity, 1, axis=1)
        laplacian = right_cell + left_cell + upper_cell + lower_cell - 4.0 * vorticity
        tendency = (
            VISCOSITY * laplacian
            - flow_x * (0.5 * (right_cell - left_cell))
            - flow_y * (0.5 * (upper_cell - lower_cell))
        )
        forcing = (
            velocity[:, 0, substep][:, None, None] * source_x
            - velocity[:, 1, substep][:, None, None] * source_y
        )
        vorticity = vorticity + TIME_STEP * tendency + COUPLING * forcing
        lift_rows.append(jnp.sum(vorticity * lift_kernel, axis=(1, 2)))
        drag_rows.append(jnp.sum(vorticity * drag_kernel, axis=(1, 2)))
    return (vorticity, jnp.stack(lift_rows + drag_rows, axis=1))


def apply_block(vectors, matrix):
    return lax.dot_general(vectors, matrix, (((1,), (1,)), ((), ())), precision=EXACT_DOT)


def first_contract(left_side, right_side):
    return lax.dot_general(left_side, right_side, (((0,), (0,)), ((), ())), precision=EXACT_DOT)


def beam_solve(beam_load, pivot_inv, lower_block, upper_block):
    block_count = pivot_inv.shape[0]
    block_size = pivot_inv.shape[1]
    blocks = beam_load.reshape(beam_load.shape[0], block_count, block_size)
    carried = [blocks[:, 0]]
    for block_index in range(1, block_count):
        pivoted = apply_block(carried[-1], pivot_inv[block_index - 1])
        carried.append(blocks[:, block_index] - apply_block(pivoted, lower_block[block_index - 1]))
    solved = [apply_block(carried[-1], pivot_inv[block_count - 1])]
    for block_index in range(block_count - 2, -1, -1):
        remainder = carried[block_index] - apply_block(solved[0], upper_block[block_index])
        solved.insert(0, apply_block(remainder, pivot_inv[block_index]))
    return jnp.concatenate(solved, axis=1)


def local(strip_fields, strip_riser, strip_node, riser_owner, pivot_inv, lower_block, upper_block):
    devices = lax.axis_size("strip")
    position = lax.axis_index("strip")
    per_device = strip_fields.shape[1]
    grid_cells = strip_fields.shape[2]
    node_count = pivot_inv.shape[1] * pivot_inv.shape[2]
    riser_count = riser_owner.shape[1]
    substeps = NSUB
    total_strips = per_device * devices * lax.axis_size("group")
    kernels = make_kernels(grid_cells)
    riser_match = (
        strip_riser[:, 0][:, None] == jnp.arange(riser_count, dtype=jnp.int32)[None, :]
    ).astype(jnp.int32)
    owner_index = jnp.sum(riser_match * riser_owner[0][None, :], axis=1)
    owned_here = owner_index == position
    node_hit = (
        owned_here[:, None]
        & (strip_node[:, None] == jnp.arange(node_count, dtype=jnp.int32)[None, :])
    ).astype(jnp.float32)
    local_owner = lax.dynamic_slice_in_dim(owner_index, position * per_device, per_device)
    local_node = lax.dynamic_slice_in_dim(strip_node, position * per_device, per_device)
    top_taper = 1.0 - jnp.arange(node_count, dtype=jnp.float32) / node_count
    vorticity = strip_fields[0]
    flow_x = strip_fields[1]
    flow_y = strip_fields[2]
    motion = jnp.zeros((per_device, 2 * substeps), jnp.float32)
    displacement = jnp.zeros((2 * substeps, node_count), jnp.float32)
    for coupled_step in range(COUPLED):
        vorticity, force_rows = strip_step(vorticity, flow_x, flow_y, motion, kernels, substeps)
        partial_drag = jnp.sum(force_rows[:, substeps:], axis=0)
        total_drag = lax.psum(partial_drag, ("group", "strip"))
        offset = total_drag / jnp.sqrt(jnp.float32(total_strips))
        beam_load = first_contract(
            lax.all_gather(force_rows, "strip", axis=0, tiled=True), node_hit
        )
        displacement = beam_solve(beam_load, pivot_inv[0], lower_block[0], upper_block[0])
        displacement = displacement.at[substeps:, :].add(offset[:, None] * top_taper[None, :])
        if coupled_step + 1 < COUPLED:
            every_owner = lax.all_gather(displacement[None], "strip", axis=0, tiled=True)
            chosen = jnp.take(every_owner, local_owner, axis=0)
            node_pick = jnp.broadcast_to(local_node[:, None, None], (per_device, 2 * substeps, 1))
            motion = jnp.take_along_axis(chosen, node_pick, axis=2)[:, :, 0]
    return (vorticity, displacement[None])


def solution(mesh):
    in_specs = (
        P(None, ("group", "strip"), None, None),
        P("group", None),
        P("group"),
        P("group", None),
        P(("group", "strip"), None, None, None),
        P(("group", "strip"), None, None, None),
        P(("group", "strip"), None, None, None),
    )
    out_specs = (P(("group", "strip"), None, None), P(("group", "strip"), None, None))
    return jax.shard_map(local, mesh=mesh, in_specs=in_specs, out_specs=out_specs, check_vma=False)
```

profile of v0, /device:TPU:0, one launch (start us, length us, event | category | flops | bytes accessed | tf_op | source)
XLA Modules:
  0.0 231.5 jit_solution(9136430588047142506)
XLA Ops:
  7.2 0.9 slice_bitcast_fusion
  8.5 0.8 copy-done
  12.4 0.7 multiply_reduce_fusion.32
  14.6 0.5 multiply_reduce_fusion.23
  15.9 42.0 %psum.14 = f32[8]{0:T(128)S(1)} all-reduce(f32[8]{0:T(128)S(1)} %reduce_sum.352), channel_id=1, replica_groups=mesh['group'=2,'strip'=16] {'group','strip'}, use_global_device_ids=true, to_apply=%region_20.21 | all-reduce | flops 8 | bytes 64 | tf_op jit(solution)/shard_map/psum | solution.py:112
  58.8 21.0 %all-gather = f32[16,2,16]{2,1,0:T(2,128)S(1)} all-gather(f32[1,2,16]{2,1,0:T(2,128)S(1)} %bitcast.564), channel_id=1, replica_groups=mesh['group'=2,'strip'=16] {'strip'}, dimensions={0}, use_global_device_ids=true | all-gather | bytes 2176 | tf_op jit(solution)/shard_map/all_gather | solution.py:115
  79.8 0.7 copy-done.6
  80.5 0.7 copy-done.5
  81.2 0.2 convolution_bitcast_fusion.1
  81.5 1.0 fusion.167
  82.5 1.1 convolution_subtract_fusion.27
  83.6 1.1 fusion.159
  84.7 1.1 convolution_subtract_fusion.26
  85.8 1.1 fusion.149
  86.9 1.1 convolution_subtract_fusion.25
  88.0 1.1 fusion.139
  89.0 1.1 convolution_subtract_fusion.24
  90.1 1.1 fusion.129
  91.2 1.1 convolution_subtract_fusion.23
  92.2 1.1 fusion.119
  93.3 1.1 convolution_subtract_fusion.22
  94.3 1.1 fusion.109
  95.4 1.1 convolution_subtract_fusion.21
  96.5 1.1 fusion.99
  98.0 0.2 convolution_subtract_fusion.19
  98.2 0.2 fusion.117
  98.4 0.2 convolution_subtract_fusion.18
  98.9 0.2 convolution_subtract_fusion.17
  99.3 0.3 convolution_subtract_fusion.16
  99.8 0.2 convolution_subtract_fusion.15
  100.2 0.3 convolution_subtract_fusion.14
  100.9 0.6 copy-done.3
  102.2 33.8 %all-gather.4.cloned.1.call-done = f32[16,16,1024]{2,1,0:T(8,128)} async-done(((f32[1,16,1024]{2,1,0:T(8,128)}), f32[16,16,1024]{2,1,0:T(8,128)}) %all-gather.4.cloned.1.call-update) | async-done | bytes 1048592 | tf_op jit(solution)/shard_map/all_gather | solution.py:120
  136.0 1.8 gather_fusion
  137.8 0.8 gather_fusion.1
  142.2 1.1 multiply_reduce_fusion.7
  144.2 38.9 %psum.15 = f32[8]{0:T(128)S(1)} all-reduce(f32[8]{0:T(128)S(1)} %reduce_sum.369), channel_id=1, replica_groups=mesh['group'=2,'strip'=16] {'group','strip'}, use_global_device_ids=true, to_apply=%region_38.39 | all-reduce | flops 8 | bytes 64 | tf_op jit(solution)/shard_map/psum | solution.py:112
  183.9 20.6 %all-gather.1 = f32[16,2,16]{2,1,0:T(2,128)S(1)} all-gather(f32[1,2,16]{2,1,0:T(2,128)S(1)} %bitcast.565), channel_id=1, replica_groups=mesh['group'=2,'strip'=16] {'strip'}, dimensions={0}, use_global_device_ids=true | all-gather | bytes 2176 | tf_op jit(solution)/shard_map/all_gather | solution.py:115
  204.5 0.2 convolution_bitcast_fusion
  204.8 1.0 fusion.164
  205.8 1.1 convolution_subtract_fusion.13
  206.9 1.1 fusion.155
  208.0 1.1 convolution_subtract_fusion.12
  209.0 1.1 fusion.145
  210.1 1.1 convolution_subtract_fusion.11
  211.2 1.1 fusion.135
  212.2 1.1 convolution_subtract_fusion.10
  213.3 1.1 fusion.125
  214.3 1.1 convolution_subtract_fusion.9
  215.4 1.1 fusion.115
  216.5 1.1 convolution_subtract_fusion.8
  217.5 1.1 fusion.105
  218.6 1.1 convolution_subtract_fusion.7
  219.6 1.1 fusion.97
  220.7 0.2 convolution_subtract_fusion.6
  220.9 0.2 fusion.103
  221.2 0.2 convolution_subtract_fusion.5
  221.4 0.2 fusion.113
  221.6 0.2 convolution_subtract_fusion.4
  222.1 0.2 convolution_subtract_fusion.3
  222.5 0.2 convolution_subtract_fusion.2
  223.0 0.2 convolution_subtract_fusion.1
  223.4 0.2 convolution_subtract_fusion
  224.1 0.6 copy-done.4
  (188 shorter events, 13.7 us)
Async XLA Ops:
  7.2 128.8 %all-gather.4.cloned.1.call-start = ((), (), s32[]{:S(2)}) async-start(), calls=%async_computation | async-start | bytes 1114112 | tf_op jit(solution)/shard_map/all_gather | solution.py:120
  8.3 1.0 copy-start
  79.8 0.7 copy-start.6
  79.8 0.7 copy-start.7
  80.5 0.7 copy-start.5
  84.7 12.9 %copy-start.2 = (f32[1,7,128,128]{3,2,1,0:T(8,128)S(1)}, f32[1,7,128,128]{3,2,1,0:T(8,128)}, u32[]{:S(2)}) copy-start(f32[1,7,128,128]{3,2,1,0:T(8,128)} %param.17) | copy-start | bytes 1376260
  85.8 12.0 %copy-start.1 = (f32[1,8,128,128]{3,2,1,0:T(8,128)S(1)}, f32[1,8,128,128]{3,2,1,0:T(8,128)}, u32[]{:S(2)}) copy-start(f32[1,8,128,128]{3,2,1,0:T(8,128)} %param.15) | copy-start | bytes 1572868
  100.9 0.6 copy-start.3
  224.1 0.6 copy-start.4
Sparse Core Ops, SparseCore 0:
  101.7 34.2 all-gather.3
where the time goes:
time: 233 us; the launch traced here: 232 us
  blocking collectives  123 us (53%)
  matrix products  38.5 us (17%)
  waiting for transfers between devices  33.8 us (15%)
  between operations  16.3 us (7%)
  local copies, waits for them, and re-layouts  14.4 us (6%)
  other arithmetic  5.94 us (3%)
    psum x2, blocking collectives, local(): total_drag = lax.psum(partial_drag, ('group', 'strip'))  80.9 us
    all_gather x2, blocking collectives, local(): lax.all_gather(force_rows, 'strip', axis=0, tiled=True)  41.6 us
    dot_general x58, matrix products, apply_block(): lax.dot_general(vectors, matrix, (((1,), (1,)), ((), ())), precision=EXAC...  38 us
    all_gather x1, waiting for transfers between devices, local(): lax.all_gather(displacement[None], 'strip', axis=0, tiled=True)  33.8 us
  transfers between devices with their start and end apart: 1, of which 1 were waited for; matrix products, arithmetic and copies ran while one was open for 0% of the time, Pallas kernels for 0%

commit v1 on v0

--- a/solution.py
+++ b/solution.py
@@ -9,6 +9,27 @@
 VISCOSITY = 0.05
 COUPLING = 0.5
 EXACT_DOT = lax.Precision.HIGHEST
+
+
+def collect(value, axis, dim):
+    peers, mine, extent = (lax.axis_size(axis), lax.axis_index(axis), value.shape[dim])
+    right = [(i, (i + 1) % peers) for i in range(peers)]
+    left = [(i, (i - 1) % peers) for i in range(peers)]
+    out = jnp.zeros((*value.shape[:dim], peers * extent, *value.shape[dim + 1 :]), value.dtype)
+    out = lax.dynamic_update_slice_in_dim(out, value, mine * extent, axis=dim)
+    from_left = from_right = value
+    halfway = peers // 2
+    for step in range(1, halfway + 1):
+        from_left = lax.ppermute(from_left, axis, right)
+        out = lax.dynamic_update_slice_in_dim(
+            out, from_left, (mine - step) % peers * extent, axis=dim
+        )
+        if step < peers - halfway:
+            from_right = lax.ppermute(from_right, axis, left)
+            out = lax.dynamic_update_slice_in_dim(
+                out, from_right, (mine + step) % peers * extent, axis=dim
+            )
+    return out
 
 
 def make_kernels(grid_cells):
@@ -111,9 +132,7 @@
         partial_drag = jnp.sum(force_rows[:, substeps:], axis=0)
         total_drag = lax.psum(partial_drag, ("group", "strip"))
         offset = total_drag / jnp.sqrt(jnp.float32(total_strips))
-        beam_load = first_contract(
-            lax.all_gather(force_rows, "strip", axis=0, tiled=True), node_hit
-        )
+        beam_load = first_contract(collect(force_rows, "strip", 0), node_hit)
         displacement = beam_solve(beam_load, pivot_inv[0], lower_block[0], upper_block[0])
         displacement = displacement.at[substeps:, :].add(offset[:, None] * top_taper[None, :])
         if coupled_step + 1 < COUPLED:

time: 233 us -> 277 us (1.19)
  starting transfers between devices: 0.04 us -> 63 us
  blocking collectives: 123 us -> 75.1 us
  waiting for transfers between devices: 33.8 us -> 62.2 us
    ppermute x0 -> x30, starting transfers between devices: none -> 63 us  [the longest x14 62 us: collect(): from_right = lax.ppermute(from_right, axis, left)]
    all_gather x2 -> x0, blocking collectives: 41.6 us -> none  [local(): lax.all_gather(force_rows, 'strip', axis=0, tiled=True)]
    ppermute x0 -> x30, waiting for transfers between devices: none -> 26.6 us  [the longest x16 26 us: collect(): from_left = lax.ppermute(from_left, axis, right)]
    psum x2, blocking collectives: 80.9 us -> 75.1 us  [local(): total_drag = lax.psum(partial_drag, ('group', 'strip'))]
  transfers between devices with their start and end apart: 1 -> 31, of which waited for: 1 -> 26; matrix products, arithmetic and copies ran while one was open for 0% -> 0% of each run, Pallas kernels for 0% -> 0%
where the time goes in v1:
time: 277 us; the launch traced here: 275 us
  blocking collectives  75.1 us (27%)
  starting transfers between devices  63 us (23%)
  waiting for transfers between devices  62.2 us (22%)
  matrix products  38.5 us (14%)
  between operations  16.7 us (6%)
  local copies, waits for them, and re-layouts  14 us (5%)
  other arithmetic  5.84 us (2%)
    psum x2, blocking collectives, local(): total_drag = lax.psum(partial_drag, ('group', 'strip'))  75.1 us
    ppermute x14, starting transfers between devices, collect(): from_right = lax.ppermute(from_right, axis, left)  62 us
    dot_general x58, matrix products, apply_block(): lax.dot_general(vectors, matrix, (((1,), (1,)), ((), ())), precision=EXAC...  38.1 us
    all_gather x1, waiting for transfers between devices, local(): lax.all_gather(displacement[None], 'strip', axis=0, tiled=True)  35.5 us
    ppermute x16, waiting for transfers between devices, collect(): from_left = lax.ppermute(from_left, axis, right)  26 us
  transfers between devices with their start and end apart: 31, of which 26 were waited for; matrix products, arithmetic and copies ran while one was open for 0% of the time, Pallas kernels for 0%

profile of v1, /device:TPU:0, one launch (start us, length us, event | category | flops | bytes accessed | tf_op | source)
XLA Modules:
  0.0 275.3 jit_solution(8888911598040440307)
XLA Ops:
  7.2 0.9 slice_bitcast_fusion
  17.1 5.1 %collective-permute-start.1 = (f32[2,16]{1,0:T(2,128)S(1)}, f32[2,16]{1,0:T(2,128)S(1)}, u32[]{:S(2)}, u32[]{:S(2)}) collective-permute-start(f32[2,16]{1,0:T(2,128)S(1)} %stack.122), channel_id=1, source_target_pairs={{0,15},{1,0},{2,1},{3,2},{4,3},{5,4},{6,5},{7,6},{8,7},{9,8},{10,9... | collective-permute-start | bytes 392 | tf_op jit(solution)/shard_map/ppermute | solution.py:28
  22.5 38.3 %psum.14 = f32[8]{0:T(128)S(1)} all-reduce(f32[8]{0:T(128)S(1)} %reduce_sum.352), channel_id=1, replica_groups=mesh['group'=2,'strip'=16] {'group','strip'}, use_global_device_ids=true, to_apply=%region_20.21 | all-reduce | flops 8 | bytes 64 | tf_op jit(solution)/shard_map/psum | solution.py:133
  61.7 4.4 %collective-permute-start.3 = (f32[2,16]{1,0:T(2,128)S(1)}, f32[2,16]{1,0:T(2,128)S(1)}, u32[]{:S(2)}, u32[]{:S(2)}) collective-permute-start(f32[2,16]{1,0:T(2,128)S(1)} %collective-permute-done.1), channel_id=1, source_target_pairs={{0,15},{1,0},{2,1},{3,2},{4,3},{5,4},{6,5},{7,6},{8,7},{9,8},{10,9... | collective-permute-start | bytes 392 | tf_op jit(solution)/shard_map/ppermute | solution.py:28
  66.1 1.2 collective-permute-done.2
  67.4 4.4 %collective-permute-start.5 = (f32[2,16]{1,0:T(2,128)S(1)}, f32[2,16]{1,0:T(2,128)S(1)}, u32[]{:S(2)}, u32[]{:S(2)}) collective-permute-start(f32[2,16]{1,0:T(2,128)S(1)} %collective-permute-done.3), channel_id=1, source_target_pairs={{0,15},{1,0},{2,1},{3,2},{4,3},{5,4},{6,5},{7,6},{8,7},{9,8},{10,9... | collective-permute-start | bytes 392 | tf_op jit(solution)/shard_map/ppermute | solution.py:28
  71.8 1.2 collective-permute-done.4
  73.1 4.4 %collective-permute-start.7 = (f32[2,16]{1,0:T(2,128)S(1)}, f32[2,16]{1,0:T(2,128)S(1)}, u32[]{:S(2)}, u32[]{:S(2)}) collective-permute-start(f32[2,16]{1,0:T(2,128)S(1)} %collective-permute-done.5), channel_id=1, source_target_pairs={{0,15},{1,0},{2,1},{3,2},{4,3},{5,4},{6,5},{7,6},{8,7},{9,8},{10,9... | collective-permute-start | bytes 392 | tf_op jit(solution)/shard_map/ppermute | solution.py:28
  77.5 1.2 collective-permute-done.6
  78.8 4.4 %collective-permute-start.9 = (f32[2,16]{1,0:T(2,128)S(1)}, f32[2,16]{1,0:T(2,128)S(1)}, u32[]{:S(2)}, u32[]{:S(2)}) collective-permute-start(f32[2,16]{1,0:T(2,128)S(1)} %collective-permute-done.7), channel_id=1, source_target_pairs={{0,15},{1,0},{2,1},{3,2},{4,3},{5,4},{6,5},{7,6},{8,7},{9,8},{10,9... | collective-permute-start | bytes 392 | tf_op jit(solution)/shard_map/ppermute | solution.py:28
  83.2 1.2 collective-permute-done.8
  84.5 4.4 %collective-permute-start.11 = (f32[2,16]{1,0:T(2,128)S(1)}, f32[2,16]{1,0:T(2,128)S(1)}, u32[]{:S(2)}, u32[]{:S(2)}) collective-permute-start(f32[2,16]{1,0:T(2,128)S(1)} %collective-permute-done.9), channel_id=1, source_target_pairs={{0,15},{1,0},{2,1},{3,2},{4,3},{5,4},{6,5},{7,6},{8,7},{9,8},{10,9... | collective-permute-start | bytes 392 | tf_op jit(solution)/shard_map/ppermute | solution.py:28
  88.9 1.2 collective-permute-done.10
  90.2 4.4 %collective-permute-start.13 = (f32[2,16]{1,0:T(2,128)S(1)}, f32[2,16]{1,0:T(2,128)S(1)}, u32[]{:S(2)}, u32[]{:S(2)}) collective-permute-start(f32[2,16]{1,0:T(2,128)S(1)} %collective-permute-done.11), channel_id=1, source_target_pairs={{0,15},{1,0},{2,1},{3,2},{4,3},{5,4},{6,5},{7,6},{8,7},{9,8},{10,9... | collective-permute-start | bytes 392 | tf_op jit(solution)/shard_map/ppermute | solution.py:28
  94.6 1.2 collective-permute-done.12
  95.9 5.6 %collective-permute-done.14 = f32[2,16]{1,0:T(2,128)S(1)} collective-permute-done((f32[2,16]{1,0:T(2,128)S(1)}, f32[2,16]{1,0:T(2,128)S(1)}, u32[]{:S(2)}, u32[]{:S(2)}) %collective-permute-start.14) | collective-permute-done | bytes 160 | tf_op jit(solution)/shard_map/ppermute | solution.py:23
  101.9 1.0 fusion.167
  102.9 1.1 convolution_subtract_fusion.27
  103.9 1.1 fusion.159
  105.0 1.1 convolution_subtract_fusion.26
  106.2 1.1 fusion.149
  107.2 1.1 convolution_subtract_fusion.25
  108.3 1.1 fusion.139
  109.4 1.1 convolution_subtract_fusion.24
  110.5 1.1 fusion.129
  111.5 1.1 convolution_subtract_fusion.23
  112.6 1.0 fusion.119
  113.6 1.1 convolution_subtract_fusion.22
  114.7 1.1 fusion.109
  115.7 1.1 convolution_subtract_fusion.21
  116.8 1.1 fusion.99
  122.5 35.5 %all-gather.2.cloned.1.call-done = f32[16,16,1024]{2,1,0:T(8,128)} async-done(((f32[1,16,1024]{2,1,0:T(8,128)}), f32[16,16,1024]{2,1,0:T(8,128)}) %all-gather.2.cloned.1.call-update) | async-done | bytes 1048592 | tf_op jit(solution)/shard_map/all_gather | solution.py:139
  158.0 1.8 gather_fusion
  164.2 1.1 multiply_reduce_fusion.7
  167.3 4.2 %collective-permute-start.16 = (f32[2,16]{1,0:T(2,128)S(1)}, f32[2,16]{1,0:T(2,128)S(1)}, u32[]{:S(2)}, u32[]{:S(2)}) collective-permute-start(f32[2,16]{1,0:T(2,128)S(1)} %stack.140), channel_id=1, source_target_pairs={{0,15},{1,0},{2,1},{3,2},{4,3},{5,4},{6,5},{7,6},{8,7},{9,8},{10,9... | collective-permute-start | bytes 392 | tf_op jit(solution)/shard_map/ppermute | solution.py:28
  171.5 36.8 %psum.15 = f32[8]{0:T(128)S(1)} all-reduce(f32[8]{0:T(128)S(1)} %reduce_sum.369), channel_id=1, replica_groups=mesh['group'=2,'strip'=16] {'group','strip'}, use_global_device_ids=true, to_apply=%region_38.39 | all-reduce | flops 8 | bytes 64 | tf_op jit(solution)/shard_map/psum | solution.py:133
  208.5 4.4 %collective-permute-start.18 = (f32[2,16]{1,0:T(2,128)S(1)}, f32[2,16]{1,0:T(2,128)S(1)}, u32[]{:S(2)}, u32[]{:S(2)}) collective-permute-start(f32[2,16]{1,0:T(2,128)S(1)} %collective-permute-done.16), channel_id=1, source_target_pairs={{0,15},{1,0},{2,1},{3,2},{4,3},{5,4},{6,5},{7,6},{8,7},{9,8},{10,9... | collective-permute-start | bytes 392 | tf_op jit(solution)/shard_map/ppermute | solution.py:28
  212.9 1.2 collective-permute-done.17
  214.2 4.4 %collective-permute-start.20 = (f32[2,16]{1,0:T(2,128)S(1)}, f32[2,16]{1,0:T(2,128)S(1)}, u32[]{:S(2)}, u32[]{:S(2)}) collective-permute-start(f32[2,16]{1,0:T(2,128)S(1)} %collective-permute-done.18), channel_id=1, source_target_pairs={{0,15},{1,0},{2,1},{3,2},{4,3},{5,4},{6,5},{7,6},{8,7},{9,8},{10,9... | collective-permute-start | bytes 392 | tf_op jit(solution)/shard_map/ppermute | solution.py:28
  218.6 1.2 collective-permute-done.19
  219.9 4.4 %collective-permute-start.22 = (f32[2,16]{1,0:T(2,128)S(1)}, f32[2,16]{1,0:T(2,128)S(1)}, u32[]{:S(2)}, u32[]{:S(2)}) collective-permute-start(f32[2,16]{1,0:T(2,128)S(1)} %collective-permute-done.20), channel_id=1, source_target_pairs={{0,15},{1,0},{2,1},{3,2},{4,3},{5,4},{6,5},{7,6},{8,7},{9,8},{10,9... | collective-permute-start | bytes 392 | tf_op jit(solution)/shard_map/ppermute | solution.py:28
  224.3 1.2 collective-permute-done.21
  225.6 4.4 %collective-permute-start.24 = (f32[2,16]{1,0:T(2,128)S(1)}, f32[2,16]{1,0:T(2,128)S(1)}, u32[]{:S(2)}, u32[]{:S(2)}) collective-permute-start(f32[2,16]{1,0:T(2,128)S(1)} %collective-permute-done.22), channel_id=1, source_target_pairs={{0,15},{1,0},{2,1},{3,2},{4,3},{5,4},{6,5},{7,6},{8,7},{9,8},{10,9... | collective-permute-start | bytes 392 | tf_op jit(solution)/shard_map/ppermute | solution.py:28
  230.0 1.2 collective-permute-done.23
  231.3 4.4 %collective-permute-start.26 = (f32[2,16]{1,0:T(2,128)S(1)}, f32[2,16]{1,0:T(2,128)S(1)}, u32[]{:S(2)}, u32[]{:S(2)}) collective-permute-start(f32[2,16]{1,0:T(2,128)S(1)} %collective-permute-done.24), channel_id=1, source_target_pairs={{0,15},{1,0},{2,1},{3,2},{4,3},{5,4},{6,5},{7,6},{8,7},{9,8},{10,9... | collective-permute-start | bytes 392 | tf_op jit(solution)/shard_map/ppermute | solution.py:28
  235.7 1.2 collective-permute-done.25
  236.9 4.4 %collective-permute-start.28 = (f32[2,16]{1,0:T(2,128)S(1)}, f32[2,16]{1,0:T(2,128)S(1)}, u32[]{:S(2)}, u32[]{:S(2)}) collective-permute-start(f32[2,16]{1,0:T(2,128)S(1)} %collective-permute-done.26), channel_id=1, source_target_pairs={{0,15},{1,0},{2,1},{3,2},{4,3},{5,4},{6,5},{7,6},{8,7},{9,8},{10,9... | collective-permute-start | bytes 392 | tf_op jit(solution)/shard_map/ppermute | solution.py:28
  241.3 1.2 collective-permute-done.27
  242.6 5.6 %collective-permute-done.29 = f32[2,16]{1,0:T(2,128)S(1)} collective-permute-done((f32[2,16]{1,0:T(2,128)S(1)}, f32[2,16]{1,0:T(2,128)S(1)}, u32[]{:S(2)}, u32[]{:S(2)}) %collective-permute-start.29) | collective-permute-done | bytes 160 | tf_op jit(solution)/shard_map/ppermute | solution.py:23
  248.6 1.0 fusion.164
  249.6 1.1 convolution_subtract_fusion.13
  250.7 1.1 fusion.155
  251.7 1.1 convolution_subtract_fusion.12
  252.8 1.1 fusion.145
  253.9 1.1 convolution_subtract_fusion.11
  254.9 1.1 fusion.135
  256.0 1.1 convolution_subtract_fusion.10
  257.1 1.1 fusion.125
  258.1 1.1 convolution_subtract_fusion.9
  259.2 1.1 fusion.115
  260.2 1.1 convolution_subtract_fusion.8
  261.3 1.1 fusion.105
  262.4 1.1 convolution_subtract_fusion.7
  263.4 1.1 fusion.97
  (280 shorter events, 24.4 us)
Async XLA Ops:
  7.2 150.8 %all-gather.2.cloned.1.call-start = ((), (), s32[]{:S(2)}) async-start(), calls=%async_computation | async-start | bytes 1114112 | tf_op jit(solution)/shard_map/all_gather | solution.py:139
  8.3 1.0 copy-start
  16.6 45.0 %collective-permute-start = (f32[2,16]{1,0:T(2,128)S(1)}, f32[2,16]{1,0:T(2,128)S(1)}, u32[]{:S(2)}, u32[]{:S(2)}) collective-permute-start(f32[2,16]{1,0:T(2,128)S(1)} %stack.122), channel_id=1, source_target_pairs={{0,1},{1,2},{2,3},{3,4},{4,5},{5,6},{6,7},{7,8},{8,9},{9,10},{10,1... | collective-permute-start | bytes 392 | tf_op jit(solution)/shard_map/ppermute | solution.py:23
  17.1 44.6 %collective-permute-start.1 = (f32[2,16]{1,0:T(2,128)S(1)}, f32[2,16]{1,0:T(2,128)S(1)}, u32[]{:S(2)}, u32[]{:S(2)}) collective-permute-start(f32[2,16]{1,0:T(2,128)S(1)} %stack.122), channel_id=1, source_target_pairs={{0,15},{1,0},{2,1},{3,2},{4,3},{5,4},{6,5},{7,6},{8,7},{9,8},{10,9... | collective-permute-start | bytes 392 | tf_op jit(solution)/shard_map/ppermute | solution.py:28
  60.7 0.7 copy-start.6
  60.7 0.7 copy-start.7
  61.6 5.7 %collective-permute-start.2 = (f32[2,16]{1,0:T(2,128)S(1)}, f32[2,16]{1,0:T(2,128)S(1)}, u32[]{:S(2)}, u32[]{:S(2)}) collective-permute-start(f32[2,16]{1,0:T(2,128)S(1)} %collective-permute-done), channel_id=1, source_target_pairs={{0,1},{1,2},{2,3},{3,4},{4,5},{5,6},{6,7},{7,8},{8,9},{9,10},{10,1... | collective-permute-start | bytes 392 | tf_op jit(solution)/shard_map/ppermute | solution.py:23
  61.7 5.7 %collective-permute-start.3 = (f32[2,16]{1,0:T(2,128)S(1)}, f32[2,16]{1,0:T(2,128)S(1)}, u32[]{:S(2)}, u32[]{:S(2)}) collective-permute-start(f32[2,16]{1,0:T(2,128)S(1)} %collective-permute-done.1), channel_id=1, source_target_pairs={{0,15},{1,0},{2,1},{3,2},{4,3},{5,4},{6,5},{7,6},{8,7},{9,8},{10,9... | collective-permute-start | bytes 392 | tf_op jit(solution)/shard_map/ppermute | solution.py:28
  67.4 5.7 %collective-permute-start.4 = (f32[2,16]{1,0:T(2,128)S(1)}, f32[2,16]{1,0:T(2,128)S(1)}, u32[]{:S(2)}, u32[]{:S(2)}) collective-permute-start(f32[2,16]{1,0:T(2,128)S(1)} %collective-permute-done.2), channel_id=1, source_target_pairs={{0,1},{1,2},{2,3},{3,4},{4,5},{5,6},{6,7},{7,8},{8,9},{9,10},{10,1... | collective-permute-start | bytes 392 | tf_op jit(solution)/shard_map/ppermute | solution.py:23
  67.4 5.7 %collective-permute-start.5 = (f32[2,16]{1,0:T(2,128)S(1)}, f32[2,16]{1,0:T(2,128)S(1)}, u32[]{:S(2)}, u32[]{:S(2)}) collective-permute-start(f32[2,16]{1,0:T(2,128)S(1)} %collective-permute-done.3), channel_id=1, source_target_pairs={{0,15},{1,0},{2,1},{3,2},{4,3},{5,4},{6,5},{7,6},{8,7},{9,8},{10,9... | collective-permute-start | bytes 392 | tf_op jit(solution)/shard_map/ppermute | solution.py:28
  73.1 5.7 %collective-permute-start.6 = (f32[2,16]{1,0:T(2,128)S(1)}, f32[2,16]{1,0:T(2,128)S(1)}, u32[]{:S(2)}, u32[]{:S(2)}) collective-permute-start(f32[2,16]{1,0:T(2,128)S(1)} %collective-permute-done.4), channel_id=1, source_target_pairs={{0,1},{1,2},{2,3},{3,4},{4,5},{5,6},{6,7},{7,8},{8,9},{9,10},{10,1... | collective-permute-start | bytes 392 | tf_op jit(solution)/shard_map/ppermute | solution.py:23
  73.1 5.7 %collective-permute-start.7 = (f32[2,16]{1,0:T(2,128)S(1)}, f32[2,16]{1,0:T(2,128)S(1)}, u32[]{:S(2)}, u32[]{:S(2)}) collective-permute-start(f32[2,16]{1,0:T(2,128)S(1)} %collective-permute-done.5), channel_id=1, source_target_pairs={{0,15},{1,0},{2,1},{3,2},{4,3},{5,4},{6,5},{7,6},{8,7},{9,8},{10,9... | collective-permute-start | bytes 392 | tf_op jit(solution)/shard_map/ppermute | solution.py:28
  78.7 5.7 %collective-permute-start.8 = (f32[2,16]{1,0:T(2,128)S(1)}, f32[2,16]{1,0:T(2,128)S(1)}, u32[]{:S(2)}, u32[]{:S(2)}) collective-permute-start(f32[2,16]{1,0:T(2,128)S(1)} %collective-permute-done.6), channel_id=1, source_target_pairs={{0,1},{1,2},{2,3},{3,4},{4,5},{5,6},{6,7},{7,8},{8,9},{9,10},{10,1... | collective-permute-start | bytes 392 | tf_op jit(solution)/shard_map/ppermute | solution.py:23
  78.8 5.7 %collective-permute-start.9 = (f32[2,16]{1,0:T(2,128)S(1)}, f32[2,16]{1,0:T(2,128)S(1)}, u32[]{:S(2)}, u32[]{:S(2)}) collective-permute-start(f32[2,16]{1,0:T(2,128)S(1)} %collective-permute-done.7), channel_id=1, source_target_pairs={{0,15},{1,0},{2,1},{3,2},{4,3},{5,4},{6,5},{7,6},{8,7},{9,8},{10,9... | collective-permute-start | bytes 392 | tf_op jit(solution)/shard_map/ppermute | solution.py:28
  84.4 5.7 %collective-permute-start.10 = (f32[2,16]{1,0:T(2,128)S(1)}, f32[2,16]{1,0:T(2,128)S(1)}, u32[]{:S(2)}, u32[]{:S(2)}) collective-permute-start(f32[2,16]{1,0:T(2,128)S(1)} %collective-permute-done.8), channel_id=1, source_target_pairs={{0,1},{1,2},{2,3},{3,4},{4,5},{5,6},{6,7},{7,8},{8,9},{9,10},{10,1... | collective-permute-start | bytes 392 | tf_op jit(solution)/shard_map/ppermute | solution.py:23
  84.5 5.7 %collective-permute-start.11 = (f32[2,16]{1,0:T(2,128)S(1)}, f32[2,16]{1,0:T(2,128)S(1)}, u32[]{:S(2)}, u32[]{:S(2)}) collective-permute-start(f32[2,16]{1,0:T(2,128)S(1)} %collective-permute-done.9), channel_id=1, source_target_pairs={{0,15},{1,0},{2,1},{3,2},{4,3},{5,4},{6,5},{7,6},{8,7},{9,8},{10,9... | collective-permute-start | bytes 392 | tf_op jit(solution)/shard_map/ppermute | solution.py:28
  90.1 5.7 %collective-permute-start.12 = (f32[2,16]{1,0:T(2,128)S(1)}, f32[2,16]{1,0:T(2,128)S(1)}, u32[]{:S(2)}, u32[]{:S(2)}) collective-permute-start(f32[2,16]{1,0:T(2,128)S(1)} %collective-permute-done.10), channel_id=1, source_target_pairs={{0,1},{1,2},{2,3},{3,4},{4,5},{5,6},{6,7},{7,8},{8,9},{9,10},{10,1... | collective-permute-start | bytes 392 | tf_op jit(solution)/shard_map/ppermute | solution.py:23
  90.2 5.7 %collective-permute-start.13 = (f32[2,16]{1,0:T(2,128)S(1)}, f32[2,16]{1,0:T(2,128)S(1)}, u32[]{:S(2)}, u32[]{:S(2)}) collective-permute-start(f32[2,16]{1,0:T(2,128)S(1)} %collective-permute-done.11), channel_id=1, source_target_pairs={{0,15},{1,0},{2,1},{3,2},{4,3},{5,4},{6,5},{7,6},{8,7},{9,8},{10,9... | collective-permute-start | bytes 392 | tf_op jit(solution)/shard_map/ppermute | solution.py:28
  95.8 5.7 %collective-permute-start.14 = (f32[2,16]{1,0:T(2,128)S(1)}, f32[2,16]{1,0:T(2,128)S(1)}, u32[]{:S(2)}, u32[]{:S(2)}) collective-permute-start(f32[2,16]{1,0:T(2,128)S(1)} %collective-permute-done.12), channel_id=1, source_target_pairs={{0,1},{1,2},{2,3},{3,4},{4,5},{5,6},{6,7},{7,8},{8,9},{9,10},{10,1... | collective-permute-start | bytes 392 | tf_op jit(solution)/shard_map/ppermute | solution.py:23
  95.9 5.6 %copy-start.5 = (s32[32]{0:T(128)S(1)}, s32[32]{0:T(128)}, u32[]{:S(2)}) copy-start(s32[32]{0:T(128)} %param.13) | copy-start | bytes 388
  105.0 12.9 %copy-start.2 = (f32[1,7,128,128]{3,2,1,0:T(8,128)S(1)}, f32[1,7,128,128]{3,2,1,0:T(8,128)}, u32[]{:S(2)}) copy-start(f32[1,7,128,128]{3,2,1,0:T(8,128)} %param.17) | copy-start | bytes 1376260
  106.1 12.0 %copy-start.1 = (f32[1,8,128,128]{3,2,1,0:T(8,128)S(1)}, f32[1,8,128,128]{3,2,1,0:T(8,128)}, u32[]{:S(2)}) copy-start(f32[1,8,128,128]{3,2,1,0:T(8,128)} %param.15) | copy-start | bytes 1572868
  121.2 0.6 copy-start.3
  167.0 41.4 %collective-permute-start.15 = (f32[2,16]{1,0:T(2,128)S(1)}, f32[2,16]{1,0:T(2,128)S(1)}, u32[]{:S(2)}, u32[]{:S(2)}) collective-permute-start(f32[2,16]{1,0:T(2,128)S(1)} %stack.140), channel_id=1, source_target_pairs={{0,1},{1,2},{2,3},{3,4},{4,5},{5,6},{6,7},{7,8},{8,9},{9,10},{10,1... | collective-permute-start | bytes 392 | tf_op jit(solution)/shard_map/ppermute | solution.py:23
  167.3 41.2 %collective-permute-start.16 = (f32[2,16]{1,0:T(2,128)S(1)}, f32[2,16]{1,0:T(2,128)S(1)}, u32[]{:S(2)}, u32[]{:S(2)}) collective-permute-start(f32[2,16]{1,0:T(2,128)S(1)} %stack.140), channel_id=1, source_target_pairs={{0,15},{1,0},{2,1},{3,2},{4,3},{5,4},{6,5},{7,6},{8,7},{9,8},{10,9... | collective-permute-start | bytes 392 | tf_op jit(solution)/shard_map/ppermute | solution.py:28
  208.4 5.7 %collective-permute-start.17 = (f32[2,16]{1,0:T(2,128)S(1)}, f32[2,16]{1,0:T(2,128)S(1)}, u32[]{:S(2)}, u32[]{:S(2)}) collective-permute-start(f32[2,16]{1,0:T(2,128)S(1)} %collective-permute-done.15), channel_id=1, source_target_pairs={{0,1},{1,2},{2,3},{3,4},{4,5},{5,6},{6,7},{7,8},{8,9},{9,10},{10,1... | collective-permute-start | bytes 392 | tf_op jit(solution)/shard_map/ppermute | solution.py:23
  208.5 5.7 %collective-permute-start.18 = (f32[2,16]{1,0:T(2,128)S(1)}, f32[2,16]{1,0:T(2,128)S(1)}, u32[]{:S(2)}, u32[]{:S(2)}) collective-permute-start(f32[2,16]{1,0:T(2,128)S(1)} %collective-permute-done.16), channel_id=1, source_target_pairs={{0,15},{1,0},{2,1},{3,2},{4,3},{5,4},{6,5},{7,6},{8,7},{9,8},{10,9... | collective-permute-start | bytes 392 | tf_op jit(solution)/shard_map/ppermute | solution.py:28
  214.1 5.7 %collective-permute-start.19 = (f32[2,16]{1,0:T(2,128)S(1)}, f32[2,16]{1,0:T(2,128)S(1)}, u32[]{:S(2)}, u32[]{:S(2)}) collective-permute-start(f32[2,16]{1,0:T(2,128)S(1)} %collective-permute-done.17), channel_id=1, source_target_pairs={{0,1},{1,2},{2,3},{3,4},{4,5},{5,6},{6,7},{7,8},{8,9},{9,10},{10,1... | collective-permute-start | bytes 392 | tf_op jit(solution)/shard_map/ppermute | solution.py:23
  214.2 5.7 %collective-permute-start.20 = (f32[2,16]{1,0:T(2,128)S(1)}, f32[2,16]{1,0:T(2,128)S(1)}, u32[]{:S(2)}, u32[]{:S(2)}) collective-permute-start(f32[2,16]{1,0:T(2,128)S(1)} %collective-permute-done.18), channel_id=1, source_target_pairs={{0,15},{1,0},{2,1},{3,2},{4,3},{5,4},{6,5},{7,6},{8,7},{9,8},{10,9... | collective-permute-start | bytes 392 | tf_op jit(solution)/shard_map/ppermute | solution.py:28
  219.8 5.7 %collective-permute-start.21 = (f32[2,16]{1,0:T(2,128)S(1)}, f32[2,16]{1,0:T(2,128)S(1)}, u32[]{:S(2)}, u32[]{:S(2)}) collective-permute-start(f32[2,16]{1,0:T(2,128)S(1)} %collective-permute-done.19), channel_id=1, source_target_pairs={{0,1},{1,2},{2,3},{3,4},{4,5},{5,6},{6,7},{7,8},{8,9},{9,10},{10,1... | collective-permute-start | bytes 392 | tf_op jit(solution)/shard_map/ppermute | solution.py:23
  219.9 5.7 %collective-permute-start.22 = (f32[2,16]{1,0:T(2,128)S(1)}, f32[2,16]{1,0:T(2,128)S(1)}, u32[]{:S(2)}, u32[]{:S(2)}) collective-permute-start(f32[2,16]{1,0:T(2,128)S(1)} %collective-permute-done.20), channel_id=1, source_target_pairs={{0,15},{1,0},{2,1},{3,2},{4,3},{5,4},{6,5},{7,6},{8,7},{9,8},{10,9... | collective-permute-start | bytes 392 | tf_op jit(solution)/shard_map/ppermute | solution.py:28
  225.5 5.7 %collective-permute-start.23 = (f32[2,16]{1,0:T(2,128)S(1)}, f32[2,16]{1,0:T(2,128)S(1)}, u32[]{:S(2)}, u32[]{:S(2)}) collective-permute-start(f32[2,16]{1,0:T(2,128)S(1)} %collective-permute-done.21), channel_id=1, source_target_pairs={{0,1},{1,2},{2,3},{3,4},{4,5},{5,6},{6,7},{7,8},{8,9},{9,10},{10,1... | collective-permute-start | bytes 392 | tf_op jit(solution)/shard_map/ppermute | solution.py:23
  225.6 5.7 %collective-permute-start.24 = (f32[2,16]{1,0:T(2,128)S(1)}, f32[2,16]{1,0:T(2,128)S(1)}, u32[]{:S(2)}, u32[]{:S(2)}) collective-permute-start(f32[2,16]{1,0:T(2,128)S(1)} %collective-permute-done.22), channel_id=1, source_target_pairs={{0,15},{1,0},{2,1},{3,2},{4,3},{5,4},{6,5},{7,6},{8,7},{9,8},{10,9... | collective-permute-start | bytes 392 | tf_op jit(solution)/shard_map/ppermute | solution.py:28
  231.2 5.7 %collective-permute-start.25 = (f32[2,16]{1,0:T(2,128)S(1)}, f32[2,16]{1,0:T(2,128)S(1)}, u32[]{:S(2)}, u32[]{:S(2)}) collective-permute-start(f32[2,16]{1,0:T(2,128)S(1)} %collective-permute-done.23), channel_id=1, source_target_pairs={{0,1},{1,2},{2,3},{3,4},{4,5},{5,6},{6,7},{7,8},{8,9},{9,10},{10,1... | collective-permute-start | bytes 392 | tf_op jit(solution)/shard_map/ppermute | solution.py:23
  231.3 5.7 %collective-permute-start.26 = (f32[2,16]{1,0:T(2,128)S(1)}, f32[2,16]{1,0:T(2,128)S(1)}, u32[]{:S(2)}, u32[]{:S(2)}) collective-permute-start(f32[2,16]{1,0:T(2,128)S(1)} %collective-permute-done.24), channel_id=1, source_target_pairs={{0,15},{1,0},{2,1},{3,2},{4,3},{5,4},{6,5},{7,6},{8,7},{9,8},{10,9... | collective-permute-start | bytes 392 | tf_op jit(solution)/shard_map/ppermute | solution.py:28
  236.9 5.7 %collective-permute-start.27 = (f32[2,16]{1,0:T(2,128)S(1)}, f32[2,16]{1,0:T(2,128)S(1)}, u32[]{:S(2)}, u32[]{:S(2)}) collective-permute-start(f32[2,16]{1,0:T(2,128)S(1)} %collective-permute-done.25), channel_id=1, source_target_pairs={{0,1},{1,2},{2,3},{3,4},{4,5},{5,6},{6,7},{7,8},{8,9},{9,10},{10,1... | collective-permute-start | bytes 392 | tf_op jit(solution)/shard_map/ppermute | solution.py:23
  236.9 5.7 %collective-permute-start.28 = (f32[2,16]{1,0:T(2,128)S(1)}, f32[2,16]{1,0:T(2,128)S(1)}, u32[]{:S(2)}, u32[]{:S(2)}) collective-permute-start(f32[2,16]{1,0:T(2,128)S(1)} %collective-permute-done.26), channel_id=1, source_target_pairs={{0,15},{1,0},{2,1},{3,2},{4,3},{5,4},{6,5},{7,6},{8,7},{9,8},{10,9... | collective-permute-start | bytes 392 | tf_op jit(solution)/shard_map/ppermute | solution.py:28
  242.6 5.7 %collective-permute-start.29 = (f32[2,16]{1,0:T(2,128)S(1)}, f32[2,16]{1,0:T(2,128)S(1)}, u32[]{:S(2)}, u32[]{:S(2)}) collective-permute-start(f32[2,16]{1,0:T(2,128)S(1)} %collective-permute-done.27), channel_id=1, source_target_pairs={{0,1},{1,2},{2,3},{3,4},{4,5},{5,6},{6,7},{7,8},{8,9},{9,10},{10,1... | collective-permute-start | bytes 392 | tf_op jit(solution)/shard_map/ppermute | solution.py:23
  267.8 0.6 copy-start.4
Sparse Core Ops, SparseCore 0:
  122.0 35.9 all-gather.1
